TPU v7x, 256 devices: a whole 4x4x8 slice. The times are simulated.
256 devices in a mesh: branch: 2 (over z_hi), head: 4 (over x), page: 32 (over y, z_lo, core).
Axes of the slice: x: 4, y: 4, z: 8 (z_hi: 2, z_lo: 4; z = z_hi * 4 + z_lo), core: 2. Of those that a mesh axis runs over, the one named last changes fastest.
Arguments:
- queries: bfloat16 [16384, 4096], P(('branch', 'page'), 'head'), may hold values from -6 to 6
- new_keys: bfloat16 [16384, 512], P(('branch', 'page'), 'head'), may hold values from -6 to 6
- new_values: bfloat16 [16384, 512], P(('branch', 'page'), 'head'), may hold values from -6 to 6
- cache_keys: bfloat16 [128, 64, 512], P(('branch', 'page'), None, 'head'), may hold values from -6 to 6
- cache_values: bfloat16 [128, 64, 512], P(('branch', 'page'), None, 'head'), may hold values from -6 to 6
- block_table: int32 [64, 32], P(('branch', 'page')), may hold values from 0 to 127, as said below
- ancestor_len: int32 [64], P(('branch', 'page')), may hold values from 256 to 2048, as said below
- out_weight: bfloat16 [4096, 8192], P('head', 'page'), may hold values from -0.375 to 0.375
Outputs:
- layer_out: bfloat16 [16384, 8192], P(('branch', 'head'), 'page')
Inputs may be any that keep to these rules, and one draw needn't show every extreme that they name: `block_table`: each row names 32 distinct page ids; its first 4 entries are the same for every branch. `ancestor_len`: every branch's ancestors fill its first 4 pages; some branch reaches the maximum.
All inputs are finite; a program needn't handle non-finite values.
Results may differ from a plain program's by a relative error of at most 0.018.
Values may be sent and summed in bfloat16 or wider, within the bound.
No kernel may reach another device: no remote copies, remote signals or barrier semaphores. Data moves between devices by JAX's collectives and lax.ppermute only.
A program may use at most 64 MiB of HBM per device.

v0:
```python
import math
import jax
import jax.numpy as jnp
from jax import lax
from jax.sharding import PartitionSpec as P

HD = 128
PAGE_TOK = 64
NEW = 256
masked_fill = -1e30


def attend(carried, queries_here, key_block, value_block, usable, score_scale):
    running_max, running_sum, accumulated = carried
    scores = (
        jnp.einsum("kbnd,jkd->kbnj", queries_here, key_block, preferred_element_type=jnp.float32)
        * score_scale
    )
    key_mask = usable[None, :, None, :]
    block_max = jnp.max(jnp.where(key_mask, scores, masked_fill), axis=-1)
    new_max = jnp.maximum(running_max, block_max)
    shrink = jnp.exp(running_max - new_max)
    weights = jnp.where(key_mask, jnp.exp(scores - new_max[..., None]), 0.0).astype(jnp.bfloat16)
    running_sum = running_sum * shrink + jnp.sum(weights.astype(jnp.float32), axis=-1)
    accumulated = accumulated * shrink[..., None] + jnp.einsum(
        "kbnj,jkd->kbnd", weights, value_block, preferred_element_type=jnp.float32
    )
    return (new_max, running_sum, accumulated)


def shards(
    queries, new_keys, new_values, cache_keys, cache_values, block_table, ancestor_len, out_weight
):
    row_count = queries.shape[0]
    branches_here = block_table.shape[0]
    slot_count = block_table.shape[1]
    heads_here = queries.shape[1] // HD
    kv_here = new_keys.shape[1] // HD
    group_size = heads_here // kv_here
    query_span = NEW * group_size
    score_scale = 1.0 / math.sqrt(HD)
    queries_here = (
        queries.reshape(branches_here, NEW, kv_here, group_size, HD)
        .transpose(2, 0, 1, 3, 4)
        .reshape(kv_here, branches_here, query_span, HD)
    )
    own_keys = new_keys.reshape(row_count, kv_here, HD)
    own_values = new_values.reshape(row_count, kv_here, HD)
    token_index = (
        jnp.arange(branches_here, dtype=jnp.int32)[:, None] * NEW
        + jnp.arange(query_span, dtype=jnp.int32)[None, :] // group_size
    )
    key_index = jnp.arange(row_count, dtype=jnp.int32)
    own_mask = (key_index[None, None, :] // NEW == token_index[:, :, None] // NEW) & (
        key_index[None, None, :] <= token_index[:, :, None]
    )
    own_scores = (
        jnp.einsum("kbnd,jkd->kbnj", queries_here, own_keys, preferred_element_type=jnp.float32)
        * score_scale
    )
    start_max = jnp.max(jnp.where(own_mask[None], own_scores, masked_fill), axis=-1)
    own_weights = jnp.where(own_mask[None], jnp.exp(own_scores - start_max[..., None]), 0.0).astype(
        jnp.bfloat16
    )
    start_sum = jnp.sum(own_weights.astype(jnp.float32), axis=-1)
    start_acc = jnp.einsum(
        "kbnj,jkd->kbnd", own_weights, own_values, preferred_element_type=jnp.float32
    )
    slot_first = jnp.arange(slot_count, dtype=jnp.int32) * PAGE_TOK
    slot_limit = jnp.clip(ancestor_len[:, None] - slot_first[None, :], 0, PAGE_TOK)
    carried = (start_max, start_sum, start_acc)
    piece_keys = lax.all_gather(cache_keys, ("branch", "page"), axis=0, tiled=True)
    piece_values = lax.all_gather(cache_values, ("branch", "page"), axis=0, tiled=True)
    page_count = piece_keys.shape[0]
    page_ids = jnp.arange(page_count, dtype=jnp.int32)
    slot_hits = block_table[:, :, None] == page_ids[None, None, :]
    live_tokens = jnp.sum(jnp.where(slot_hits, slot_limit[:, :, None], 0), axis=1)
    usable = jnp.arange(PAGE_TOK, dtype=jnp.int32)[None, None, :] < live_tokens[:, :, None]
    key_total = page_count * PAGE_TOK
    block_len = math.gcd(key_total, 512)
    block_count = key_total // block_len
    key_blocks = piece_keys.reshape(block_count, block_len, kv_here, HD)
    value_blocks = piece_values.reshape(block_count, block_len, kv_here, HD)
    usable_blocks = usable.reshape(branches_here, block_count, block_len).transpose(1, 0, 2)

    def block_step(state, block_item):
        key_block, value_block, usable_block = block_item
        state = attend(state, queries_here, key_block, value_block, usable_block, score_scale)
        return (state, None)

    carried, _ = lax.scan(block_step, carried, (key_blocks, value_blocks, usable_blocks))
    final_max, final_sum, final_acc = carried
    attn_out = (final_acc / final_sum[..., None]).reshape(
        kv_here, branches_here, NEW, group_size, HD
    )
    attn_out = (
        attn_out.transpose(1, 2, 0, 3, 4).reshape(row_count, heads_here * HD).astype(jnp.bfloat16)
    )
    partial_term = jnp.dot(
        lax.all_gather(attn_out, "page", axis=0, tiled=True),
        out_weight,
        preferred_element_type=jnp.float32,
    ).astype(jnp.bfloat16)
    summed = lax.psum_scatter(
        partial_term.astype(jnp.float32).astype(jnp.bfloat16),
        "head",
        scatter_dimension=0,
        tiled=True,
    )
    return summed


def solution(mesh):
    in_specs = (
        P(("branch", "page"), "head"),
        P(("branch", "page"), "head"),
        P(("branch", "page"), "head"),
        P(("branch", "page"), None, "head"),
        P(("branch", "page"), None, "head"),
        P(("branch", "page"), None),
        P(("branch", "page")),
        P("head", "page"),
    )
    out_specs = P(("branch", "head"), "page")
    return jax.shard_map(shards, mesh=mesh, in_specs=in_specs, out_specs=out_specs, check_vma=False)
```

profile of v0, /device:TPU:1, one launch (start us, length us, event | category | flops | bytes accessed | tf_op | source)
XLA Modules:
  0.0 490.3 jit_solution(336189161934628019)
XLA Ops:
  15.0 112.1 %all-gather.4.cloned.1.call-done = bf16[128,64,128]{2,1,0:T(8,128)(2,1)} async-done(((bf16[2,64,128]{2,1,0:T(8,128)(2,1)}), bf16[128,64,128]{2,1,0:T(8,128)(2,1)}) %all-gather.4.cloned.1.call-update) | async-done | bytes 2097168 | tf_op jit(solution)/shard_map/all_gather | solution.py:72
  127.1 114.1 %all-gather.6.cloned.1.call-done = bf16[128,64,128]{2,1,0:T(8,128)(2,1)} async-done(((bf16[2,64,128]{2,1,0:T(8,128)(2,1)}), bf16[128,64,128]{2,1,0:T(8,128)(2,1)}) %all-gather.6.cloned.1.call-update) | async-done | bytes 2097168 | tf_op jit(solution)/shard_map/all_gather | solution.py:73
  241.2 80.6 %while.14 = (s32[]{:T(128)}, f32[1,1,2048]{2,1,0:T(1,128)S(1)}, f32[1,1,2048]{2,1,0:T(1,128)S(1)}, f32[1,1,2048,128]{3,2,1,0:T(8,128)S(1)}, pred[16,1,512]{2,0,1...) while((s32[]{:T(128)}, f32[1,1,2048]{2,1,0:T(1,128)S(1)}, ...), condition=%wide.region_6.7_spmd, body=%wide.region_3.6_spmd.sunk | while | flops 551030784 | bytes 15600241 | solution.py:91
  241.3 1.6 select_reduce_fusion.4
  243.8 2.4 fusion.24
  248.9 2.4 fusion.24
  251.3 1.6 select_reduce_fusion.4
  253.9 2.4 fusion.24
  258.9 2.4 fusion.24
  264.0 2.4 fusion.24
  269.0 2.4 fusion.24
  274.1 2.4 fusion.24
  279.1 2.4 fusion.24
  284.1 2.4 fusion.24
  289.2 2.4 fusion.24
  294.2 2.4 fusion.24
  299.2 2.4 fusion.24
  304.3 2.4 fusion.24
  309.3 2.4 fusion.24
  314.3 2.4 fusion.24
  319.4 2.4 fusion.24
  323.3 98.4 %all-gather.8.cloned.1.call-done = bf16[8192,1024]{1,0:T(8,128)(2,1)} async-done(((bf16[256,1024]{1,0:T(8,128)(2,1)}), bf16[8192,1024]{1,0:T(8,128)(2,1)}) %all-gather.8.cloned.1.call-update) | async-done | bytes 16777232 | tf_op jit(solution)/shard_map/all_gather | solution.py:100
  421.6 12.2 %convolution_convert_fusion = bf16[8192,256]{1,0:T(8,128)(2,1)} fusion(bf16[8192,1024]{1,0:T(8,128)(2,1)} %all-gather.8.cloned.1.call-done, bf16[1024,256]{1,0:T(8,128)(2,1)S(1)} %copy-done), kind=kOutput, calls=%fused_computation.16 | convolution fusion | flops 4297064448 | bytes 21495808 | tf_op jit(solution)/shard_map/dot_general | solution.py:99
  433.9 49.9 %reduce-scatter.2.cloned.1.call-done = bf16[2048,256]{1,0:T(8,128)(2,1)} async-done(((bf16[8192,256]{1,0:T(8,128)(2,1)}), bf16[2048,256]{1,0:T(8,128)(2,1)}) %reduce-scatter.2.cloned.1.call-update) | async-done | bytes 1048592 | tf_op jit(solution)/shard_map/reduce_scatter | solution.py:104
  (122 shorter events, 47.1 us)
Async XLA Ops:
  6.5 415.1 %copy-start = (bf16[1024,256]{1,0:T(8,128)(2,1)S(1)}, bf16[1024,256]{1,0:T(8,128)(2,1)}, u32[]{:S(2)}) copy-start(bf16[1024,256]{1,0:T(8,128)(2,1)} %param.17) | copy-start | bytes 1572868
  6.5 120.6 %all-gather.4.cloned.1.call-start = ((), (), s32[]{:S(2)}) async-start(), calls=%async_computation.1 | async-start | bytes 2129920 | tf_op jit(solution)/shard_map/all_gather | solution.py:72
  7.3 234.0 %all-gather.6.cloned.1.call-start = ((), (), s32[]{:S(2)}) async-start(), calls=%async_computation.2 | async-start | bytes 2129920 | tf_op jit(solution)/shard_map/all_gather | solution.py:73
  8.0 413.6 %all-gather.8.cloned.1.call-start = ((), (), s32[]{:S(2)}) async-start(), calls=%async_computation.3 | async-start | bytes 17301504 | tf_op jit(solution)/shard_map/all_gather | solution.py:100
  9.3 5.2 %copy-start.1 = (bf16[256,128]{1,0:T(8,128)(2,1)S(1)}, bf16[256,128]{1,0:T(8,128)(2,1)}, u32[]{:S(2)}) copy-start(bf16[256,128]{1,0:T(8,128)(2,1)} %param.12) | copy-start | bytes 196612
  323.2 160.6 %reduce-scatter.2.cloned.1.call-start = ((), (), s32[]{:S(2)}) async-start(), calls=%async_computation.4 | async-start | bytes 5242880 | tf_op jit(solution)/shard_map/reduce_scatter | solution.py:104
Sparse Core Ops, SparseCore 0:
  9.2 117.8 all-gather.3
  129.0 112.2 all-gather.5
  323.3 98.2 all-gather.7
  434.0 49.7 reduce-scatter.1
where the time goes:
time: 491 us; the launch traced here: 490 us
  waiting for transfers between devices  376 us (77%)
  matrix products  79 us (16%)
  other arithmetic  16.3 us (3%)
  between operations  13.8 us (3%)
    all_gather x1, waiting for transfers between devices, shards(): lax.all_gather(cache_values, ('branch', 'page'), axis=0, tiled=True)  114 us
    all_gather x1, waiting for transfers between devices, shards(): lax.all_gather(cache_keys, ('branch', 'page'), axis=0, tiled=True)  112 us
    all_gather x1, waiting for transfers between devices, shards(): lax.all_gather(attn_out, 'page', axis=0, tiled=True)  98.4 us
    reduce_scatter x1, waiting for transfers between devices, shards(): lax.psum_scatter(partial_term.astype(jnp.float32).astype(jnp.bfloat16), '...  49.9 us
    dot_general x16, matrix products, attend(): jnp.einsum('kbnj,jkd->kbnd', weights, value_block, preferred_element_type...  38.5 us
    dot_general x16, matrix products, attend(): jnp.einsum('kbnd,jkd->kbnj', queries_here, key_block, preferred_element_t...  26.3 us
    reduce_sum x16, other arithmetic, attend(): jnp.sum(weights.astype(jnp.float32), axis=-1)  13.8 us
    dot_general x1, matrix products, shards(): jnp.dot(lax.all_gather(attn_out, 'page', axis=0, tiled=True), out_weight,...  12.2 us
  transfers between devices with their start and end apart: 4, of which 4 were waited for; matrix products, arithmetic and copies ran while one was open for 1% of the time, Pallas kernels for 0%

commit v1 on v0

--- a/solution.py
+++ b/solution.py
@@ -70,7 +70,12 @@
     slot_limit = jnp.clip(ancestor_len[:, None] - slot_first[None, :], 0, PAGE_TOK)
     carried = (start_max, start_sum, start_acc)
     piece_keys = lax.all_gather(cache_keys, ("branch", "page"), axis=0, tiled=True)
-    piece_values = lax.all_gather(cache_values, ("branch", "page"), axis=0, tiled=True)
+    piece_values = jnp.concatenate(
+        lax.all_to_all(
+            jnp.stack([cache_values] * lax.axis_size(("branch", "page"))), ("branch", "page"), 0, 0
+        ),
+        axis=0,
+    )
     page_count = piece_keys.shape[0]
     page_ids = jnp.arange(page_count, dtype=jnp.int32)
     slot_hits = block_table[:, :, None] == page_ids[None, None, :]

time: 491 us -> 386 us (0.79)
  waiting for transfers between devices: 376 us -> 258 us
  starting transfers between devices: 0.12 us -> 13.6 us
    all_gather x1 -> x0, waiting for transfers between devices: 114 us -> none  [shards(): lax.all_gather(cache_values, ('branch', 'page'), axis=0, tiled=True)]
    all_to_all x0 -> x1, starting transfers between devices: none -> 13.3 us  [shards(): lax.all_to_all(jnp.stack([cache_values] * lax.axis_size(('branch', 'page'...]
  transfers between devices with their start and end apart: 4 -> 4, of which waited for: 4 -> 3; matrix products, arithmetic and copies ran while one was open for 1% -> 1% of each run, Pallas kernels for 0% -> 0%
where the time goes in v1:
time: 386 us; the launch traced here: 385 us
  waiting for transfers between devices  258 us (67%)
  matrix products  78.2 us (20%)
  other arithmetic  15.6 us (4%)
  between operations  13.9 us (4%)
  starting transfers between devices  13.6 us (4%)
  local copies, waits for them, and re-layouts  4.85 us (1%)
    all_gather x1, waiting for transfers between devices, shards(): lax.all_gather(cache_keys, ('branch', 'page'), axis=0, tiled=True)  107 us
    all_gather x1, waiting for transfers between devices, shards(): lax.all_gather(attn_out, 'page', axis=0, tiled=True)  100 us
    reduce_scatter x1, waiting for transfers between devices, shards(): lax.psum_scatter(partial_term.astype(jnp.float32).astype(jnp.bfloat16), '...  49.9 us
    dot_general x16, matrix products, attend(): jnp.einsum('kbnj,jkd->kbnd', weights, value_block, preferred_element_type...  38.5 us
    dot_general x16, matrix products, attend(): jnp.einsum('kbnd,jkd->kbnj', queries_here, key_block, preferred_element_t...  26.3 us
    reduce_sum x16, other arithmetic, attend(): jnp.sum(weights.astype(jnp.float32), axis=-1)  13.8 us
    all_to_all x1, starting transfers between devices, shards(): lax.all_to_all(jnp.stack([cache_values] * lax.axis_size(('branch', 'page'...  13.3 us
    dot_general x1, matrix products, shards(): jnp.dot(lax.all_gather(attn_out, 'page', axis=0, tiled=True), out_weight,...  12.2 us
  transfers between devices with their start and end apart: 4, of which 3 were waited for; matrix products, arithmetic and copies ran while one was open for 1% of the time, Pallas kernels for 0%

profile of v1, /device:TPU:1, one launch (start us, length us, event | category | flops | bytes accessed | tf_op | source)
XLA Modules:
  0.0 385.2 jit_solution(11456399077432349465)
XLA Ops:
  7.3 2.6 stack.2
  9.9 13.3 %all-to-all-start = ((bf16[64,2,64,128]{3,2,1,0:T(8,128)(2,1)}), bf16[64,2,64,128]{3,2,1,0:T(8,128)(2,1)}, u32[]{:S(2)}, u32[]{:S(2)}) async-start(bf16[64,2,64,128]{3,2,1,0:T(8,128)(2,1)} %stack.2), calls=%async_computation | async-start | bytes 4194304 | tf_op jit(solution)/shard_map/all_to_all | solution.py:74
  26.7 107.3 %all-gather.3.cloned.1.call-done = bf16[128,64,128]{2,1,0:T(8,128)(2,1)} async-done(((bf16[2,64,128]{2,1,0:T(8,128)(2,1)}), bf16[128,64,128]{2,1,0:T(8,128)(2,1)}) %all-gather.3.cloned.1.call-update) | async-done | bytes 2097168 | tf_op jit(solution)/shard_map/all_gather | solution.py:72
  134.0 80.6 %while.14 = (s32[]{:T(128)}, f32[1,1,2048]{2,1,0:T(1,128)S(1)}, f32[1,1,2048]{2,1,0:T(1,128)S(1)}, f32[1,1,2048,128]{3,2,1,0:T(8,128)S(1)}, pred[16,1,512]{2,0,1...) while((s32[]{:T(128)}, f32[1,1,2048]{2,1,0:T(1,128)S(1)}, ...), condition=%wide.region_6.7_spmd, body=%wide.region_3.6_spmd.sunk | while | flops 551030784 | bytes 15600241 | solution.py:96
  136.6 2.4 fusion.24
  139.1 1.6 select_reduce_fusion.4
  141.7 2.4 fusion.24
  146.7 2.4 fusion.24
  151.7 2.4 fusion.24
  156.8 2.4 fusion.24
  161.8 2.4 fusion.24
  166.8 2.4 fusion.24
  171.9 2.4 fusion.24
  176.9 2.4 fusion.24
  182.0 2.4 fusion.24
  187.0 2.4 fusion.24
  192.0 2.4 fusion.24
  197.1 2.4 fusion.24
  202.1 2.4 fusion.24
  207.1 2.4 fusion.24
  212.2 2.4 fusion.24
  216.2 100.3 %all-gather.5.cloned.1.call-done = bf16[8192,1024]{1,0:T(8,128)(2,1)} async-done(((bf16[256,1024]{1,0:T(8,128)(2,1)}), bf16[8192,1024]{1,0:T(8,128)(2,1)}) %all-gather.5.cloned.1.call-update) | async-done | bytes 16777232 | tf_op jit(solution)/shard_map/all_gather | solution.py:105
  316.5 12.2 %convolution_convert_fusion = bf16[8192,256]{1,0:T(8,128)(2,1)} fusion(bf16[8192,1024]{1,0:T(8,128)(2,1)} %all-gather.5.cloned.1.call-done, bf16[1024,256]{1,0:T(8,128)(2,1)S(1)} %copy-done), kind=kOutput, calls=%fused_computation.16 | convolution fusion | flops 4297064448 | bytes 21495808 | tf_op jit(solution)/shard_map/dot_general | solution.py:104
  328.8 49.9 %reduce-scatter.2.cloned.1.call-done = bf16[2048,256]{1,0:T(8,128)(2,1)} async-done(((bf16[8192,256]{1,0:T(8,128)(2,1)}), bf16[2048,256]{1,0:T(8,128)(2,1)}) %reduce-scatter.2.cloned.1.call-update) | async-done | bytes 1048592 | tf_op jit(solution)/shard_map/reduce_scatter | solution.py:109
  (128 shorter events, 44.6 us)
Async XLA Ops:
  6.5 310.0 %copy-start = (bf16[1024,256]{1,0:T(8,128)(2,1)S(1)}, bf16[1024,256]{1,0:T(8,128)(2,1)}, u32[]{:S(2)}) copy-start(bf16[1024,256]{1,0:T(8,128)(2,1)} %param.17) | copy-start | bytes 1572868
  6.5 16.8 %copy-start.1 = (bf16[256,1024]{1,0:T(8,128)(2,1)S(1)}, bf16[256,1024]{1,0:T(8,128)(2,1)}, u32[]{:S(2)}) copy-start(bf16[256,1024]{1,0:T(8,128)(2,1)} %param.10) | copy-start | bytes 1572868
  6.5 127.5 %all-gather.3.cloned.1.call-start = ((), (), s32[]{:S(2)}) async-start(), calls=%async_computation.2 | async-start | bytes 2129920 | tf_op jit(solution)/shard_map/all_gather | solution.py:72
  7.3 17.3 %copy-start.4 = (s32[1,32]{1,0:T(1,128)S(1)}, s32[1,32]{1,0:T(1,128)}, u32[]{:S(2)}) copy-start(s32[1,32]{1,0:T(1,128)} %param.15) | copy-start | bytes 388
  7.3 17.5 %copy-start.3 = (bf16[256,128]{1,0:T(8,128)(2,1)S(1)}, bf16[256,128]{1,0:T(8,128)(2,1)}, u32[]{:S(2)}) copy-start(bf16[256,128]{1,0:T(8,128)(2,1)} %param.11) | copy-start | bytes 196612
  9.9 124.1 %all-to-all-start = ((bf16[64,2,64,128]{3,2,1,0:T(8,128)(2,1)}), bf16[64,2,64,128]{3,2,1,0:T(8,128)(2,1)}, u32[]{:S(2)}, u32[]{:S(2)}) async-start(bf16[64,2,64,128]{3,2,1,0:T(8,128)(2,1)} %stack.2), calls=%async_computation | async-start | bytes 4194304 | tf_op jit(solution)/shard_map/all_to_all | solution.py:74
  23.3 293.2 %all-gather.5.cloned.1.call-start = ((), (), s32[]{:S(2)}) async-start(), calls=%async_computation.3 | async-start | bytes 17301504 | tf_op jit(solution)/shard_map/all_gather | solution.py:105
  23.5 2.7 copy-start.2
  216.0 162.7 %reduce-scatter.2.cloned.1.call-start = ((), (), s32[]{:S(2)}) async-start(), calls=%async_computation.4 | async-start | bytes 5242880 | tf_op jit(solution)/shard_map/reduce_scatter | solution.py:109
Sparse Core Ops, SparseCore 0:
  9.2 124.7 all-gather.2
  216.1 100.3 all-gather.4
  328.9 49.7 reduce-scatter.1
